TPU v7x, 512 devices: a whole 4x8x8 slice. The times are simulated.
512 devices in a mesh: req: 64 (over x, y, core), head: 8 (over z).
Axes of the slice: x: 4, y: 8, z: 8, core: 2. Of those that a mesh axis runs over, the one named last changes fastest.
Arguments:
- queries: bfloat16 [2, 64, 128, 576], P(None, 'req', 'head'), may hold values from -100 to 100
- prompt_cache: bfloat16 [32768, 576], P('req'), may hold values from -10 to 10
- suffix_cache: bfloat16 [64, 8, 64, 576], P('req'), may hold values from -14 to 14
- new_latent: bfloat16 [2, 64, 576], P(None, 'req'), may hold values from -16 to 16
- suffix_len: int32 [64], P('req'), may hold values from 1 to 512, 16640 in all
- parent: int32 [64], P('req'), may hold values from 0 to 63
- fork_pages: int32 [64, 2], P('req'), may hold values from 0 to 7
Outputs:
- attended: bfloat16 [2, 64, 128, 512], P(None, 'req', 'head')
Inputs may be any that keep to these rules, and one draw needn't show every extreme that they name: `suffix_len`: every beam has at least one valid own token.
All inputs are finite; a program needn't handle non-finite values. No bound on the sum of `suffix_len` on one device may be relied on, other than what follows from the above.
Results may differ from a plain program's by a relative error of at most 0.008.
Values may be sent and summed in bfloat16 or wider, within the bound.
No kernel may reach another device: no remote copies, remote signals or barrier semaphores. Data moves between devices by JAX's collectives and lax.ppermute only.
A program may use at most 64 MiB of HBM per device.

v0:
```python
import math
import jax
import jax.numpy as jnp
from jax import lax
from jax.sharding import PartitionSpec as P

DL = 512
score_scale = 192.0 ** (-0.5)
neg_large = -1e30


def prompt_block(rows, keys):
    scores = (
        lax.dot_general(rows, keys, (((1,), (1,)), ((), ())), preferred_element_type=jnp.float32)
        * score_scale
    )
    top = jnp.max(scores, axis=-1)
    weights = jnp.exp(scores - top[:, None])
    total = jnp.sum(weights, axis=-1)
    summed = jnp.dot(weights.astype(jnp.bfloat16), keys[:, :DL], preferred_element_type=jnp.float32)
    return (top, total, (summed / total[:, None]).astype(jnp.bfloat16))


def masked_partial(queries, keys, valid):
    scores = (
        jnp.einsum("sbhk,btk->sbht", queries, keys, preferred_element_type=jnp.float32)
        * score_scale
    )
    scores = jnp.where(valid, scores, neg_large)
    top = jnp.max(scores, axis=-1)
    weights = jnp.where(valid, jnp.exp(scores - top[..., None]), 0.0)
    total = jnp.sum(weights, axis=-1)
    summed = jnp.einsum(
        "sbht,btd->sbhd",
        weights.astype(jnp.bfloat16),
        keys[..., :DL],
        preferred_element_type=jnp.float32,
    )
    return (top, total, summed)


def finish_fork(total, summed):
    return (summed / jnp.maximum(total, 1.0)[..., None]).astype(jnp.bfloat16)


def combine_parts(top_pr, total_pr, out_pr, top_fr, total_fr, out_fr, top_l, total_l, summed_l):
    peak = jnp.maximum(jnp.maximum(jnp.max(top_pr, axis=1), jnp.max(top_fr, axis=1)), top_l)
    weight_p = total_pr * jnp.exp(top_pr - peak[:, None])
    weight_f = total_fr * jnp.exp(top_fr - peak[:, None])
    weight_l = jnp.exp(top_l - peak)
    denom = jnp.sum(weight_p, axis=1) + jnp.sum(weight_f, axis=1) + total_l * weight_l
    numer = (
        jnp.sum(weight_p[..., None] * out_pr, axis=1)
        + jnp.sum(weight_f[..., None] * out_fr, axis=1)
        + weight_l[..., None] * summed_l
    )
    return numer / denom[..., None]


def on_device(queries, prompt_cache, suffix_cache, new_latent, suffix_len, parent, fork_pages):
    steps_n, beam_dev, head_dev, width = queries.shape
    pages_n, page_len = (suffix_cache.shape[1], suffix_cache.shape[2])
    forks_n = fork_pages.shape[1]
    req_n = lax.axis_size("req")
    first_beam = lax.axis_index("req") * beam_dev
    every_query = lax.all_gather(queries, "req", axis=1, tiled=True)
    all_parent, all_pages, all_len = (
        lax.all_gather(parent, "req", axis=0, tiled=True),
        lax.all_gather(fork_pages, "req", axis=0, tiled=True),
        lax.all_gather(suffix_len, "req", axis=0, tiled=True),
    )
    beams_n = every_query.shape[1]
    rows_n = steps_n * beams_n * head_dev
    block = math.gcd(rows_n, 512)
    blocks = every_query.reshape(rows_n // block, block, width)
    top_p, total_p, out_p = lax.map(lambda rows: prompt_block(rows, prompt_cache), blocks)
    top_p = top_p.reshape(steps_n, beams_n, head_dev)
    total_p = total_p.reshape(steps_n, beams_n, head_dev)
    out_p = out_p.reshape(steps_n, beams_n, head_dev, DL)
    local_parent = all_parent - first_beam
    owned = (local_parent >= 0) & (local_parent < beam_dev)
    source_beam = jnp.clip(local_parent, 0, beam_dev - 1)
    picked = suffix_cache[source_beam[:, None], all_pages]
    offsets = jnp.arange(page_len, dtype=jnp.int32)
    own_keys = jnp.concatenate(
        [suffix_cache.reshape(beam_dev, pages_n * page_len, width), jnp.swapaxes(new_latent, 0, 1)],
        axis=1,
    )
    old_valid = jnp.arange(pages_n * page_len, dtype=jnp.int32)[None, :] < suffix_len[:, None]
    new_valid = (
        jnp.arange(steps_n, dtype=jnp.int32)[None, :]
        <= jnp.arange(steps_n, dtype=jnp.int32)[:, None]
    )
    own_valid = jnp.concatenate(
        [
            jnp.broadcast_to(old_valid[None], (steps_n, beam_dev, pages_n * page_len)),
            new_valid[:, None, :],
        ],
        axis=2,
    )[:, :, None, :]
    top_l, total_l, summed_l = masked_partial(queries, own_keys, own_valid)
    outgoing = jnp.where(owned[:, None, None, None], picked, jnp.zeros_like(picked))
    arrived = lax.all_to_all(outgoing, "req", split_axis=0, concat_axis=0, tiled=True)
    tiles = jnp.sum(arrived.reshape(req_n, beam_dev, forks_n, page_len, width), axis=0)
    tiles = tiles.reshape(beam_dev, forks_n * page_len, width)
    positions = (fork_pages[:, :, None] * page_len + offsets[None, None, :]).reshape(beam_dev, -1)
    fork_valid = (positions < all_len[parent][:, None])[None, :, None, :]
    top_f, total_f, summed_f = masked_partial(queries, tiles, fork_valid)
    out_f = finish_fork(total_f, summed_f).astype(jnp.float32)
    out_pr, top_pr, total_pr = (
        lax.all_to_all(
            out_p.astype(jnp.float32), "req", split_axis=1, concat_axis=1, tiled=True
        ).astype(out_p.dtype),
        lax.all_to_all(top_p, "req", split_axis=1, concat_axis=1, tiled=True),
        lax.all_to_all(total_p, "req", split_axis=1, concat_axis=1, tiled=True),
    )
    top_pr = top_pr.reshape(steps_n, req_n, beam_dev, head_dev)
    total_pr = total_pr.reshape(steps_n, req_n, beam_dev, head_dev)
    out_pr = out_pr.astype(jnp.float32).reshape(steps_n, req_n, beam_dev, head_dev, DL)
    result = combine_parts(
        top_pr,
        total_pr,
        out_pr,
        top_f[:, None],
        total_f[:, None],
        out_f[:, None],
        top_l,
        total_l,
        summed_l,
    )
    return result.astype(jnp.bfloat16)


def solution(mesh):
    placed = (
        P(None, "req", "head", None),
        P("req", None),
        P("req", None, None, None),
        P(None, "req", None),
        P("req"),
        P("req"),
        P("req", None),
    )
    return jax.shard_map(
        on_device,
        mesh=mesh,
        in_specs=placed,
        out_specs=P(None, "req", "head", None),
        check_vma=False,
    )
```

profile of v0, /device:TPU:1, one launch (start us, length us, event | category | flops | bytes accessed | tf_op | source)
XLA Modules:
  0.0 454.0 jit_solution(4871701999400987592)
XLA Ops:
  6.5 0.7 all-gather.3.cloned.1.call-update
  8.6 39.9 %all-gather = s32[64,1,2]{2,1,0:T(1,128)S(1)} all-gather(s32[1,1,2]{2,1,0:T(1,128)} %bitcast.151), channel_id=1, replica_groups=mesh['req'=64,'head'=8] {'req'}, dimensions={0}, use_global_device_ids=true | all-gather | bytes 520 | tf_op jit(solution)/shard_map/all_gather | solution.py:69
  48.5 0.1 copy.24
  48.5 1.3 dynamic-slice.3
  49.9 0.7 dynamic-update-slice.2
  50.6 0.7 dynamic-update-slice.1
  51.4 13.4 %all-reduce.2 = (s32[64]{0:T(128)S(1)}, s32[64]{0:T(128)S(1)}) all-reduce(s32[64]{0:T(128)S(1)} %dynamic-update-slice.2, s32[64]{0:T(128)S(1)} %dynamic-update-slice.1), channel_id=1, replica_groups=mesh['req'=64,'head'=8] {'req'}, use_global_device_ids=true, to_apply=%add.1 | all-reduce | flops 128 | bytes 1024
  64.8 34.7 %all-gather.3.cloned.1.call-done = bf16[2,64,16,576]{3,2,1,0:T(8,128)(2,1)} async-done(((bf16[2,1,16,576]{3,2,1,0:T(8,128)(2,1)}), bf16[2,64,16,576]{3,2,1,0:T(8,128)(2,1)}) %all-gather.3.cloned.1.call-update) | async-done | bytes 2359312 | tf_op jit(solution)/shard_map/all_gather | solution.py:66
  99.5 11.2 %while.15 = (s32[]{:T(128)}, f32[4,512]{1,0:T(4,128)S(1)}, f32[4,512]{1,0:T(4,128)S(1)}, bf16[4,512,512]{2,1,0:T(8,128)(2,1)S(1)}, bf16[4,512,576]{2,1,0:T(8,128...) while((s32[]{:T(128)}, f32[4,512]{1,0:T(4,128)S(1)}, f32[4,512]{1,0:T(4,128)S(1)}, ...), condition=%wide.region_3.4_spmd, body=%wide.region_0.3_spmd.sunk | while | flops 572521472 | bytes 7817853 | solution.py:76
  99.5 2.0 fusion.73
  101.5 0.2 fusion.74
  101.7 0.5 fusion.75
  102.2 0.1 dynamic_update_slice.17
  102.3 0.1 dynamic_update_slice.16
  102.3 0.0 copy-start.1
  102.4 2.0 fusion.73
  104.3 0.2 fusion.74
  104.5 0.5 fusion.75
  105.0 0.1 dynamic_update_slice.17
  105.1 0.1 dynamic_update_slice.16
  105.2 0.0 copy-start.1
  105.2 2.0 fusion.73
  107.1 0.2 fusion.74
  107.3 0.5 fusion.75
  107.8 0.1 dynamic_update_slice.17
  107.9 0.1 dynamic_update_slice.16
  108.0 0.0 copy-start.1
  108.0 2.0 fusion.73
  109.9 0.2 fusion.74
  110.1 0.5 fusion.75
  110.7 0.1 dynamic_update_slice.17
  110.7 0.1 dynamic_update_slice.16
  110.8 0.1 reshape.289
  110.9 0.7 copy.23
  111.5 6.5 %all-to-all-start.1 = ((f32[2,64,16]{2,0,1:T(2,128)}), f32[2,64,16]{2,0,1:T(2,128)S(1)}, u32[]{:S(2)}, u32[]{:S(2)}) async-start(f32[2,64,16]{2,0,1:T(2,128)} %copy.23), calls=%async_computation.1 | async-start | bytes 131072 | tf_op jit(solution)/shard_map/all_to_all | solution.py:114
  118.1 0.1 copy.25
  118.2 0.1 reshape.321
  118.3 7.9 %gather_fusion = bf16[128,64,576]{2,1,0:T(8,128)(2,1)} fusion(bf16[1,8,64,576]{3,2,1,0:T(8,128)(2,1)S(1)} %copy-done, s32[128]{0:T(128)S(1)} %reshape.321), kind=kCustom, calls=%fused_computation | custom fusion | bytes 18875392 | tf_op jit(solution)/shard_map/gather | solution.py:83
  126.2 0.1 reshape.288
  126.3 0.7 copy.22
  127.0 0.9 all-to-all-done.1
  127.9 9.4 %all-to-all-start = ((f32[2,64,16]{2,0,1:T(2,128)}), f32[2,64,16]{2,0,1:T(2,128)S(1)}, u32[]{:S(2)}, u32[]{:S(2)}) async-start(f32[2,64,16]{2,0,1:T(2,128)} %copy.22), calls=%async_computation | async-start | bytes 131072 | tf_op jit(solution)/shard_map/all_to_all | solution.py:115
  137.3 10.0 %broadcast_select_fusion = bf16[64,2,64,576]{3,2,1,0:T(8,128)(2,1)} fusion(bf16[64,2,64,576]{3,2,1,0:T(8,128)(2,1)} %bitcast.144, pred[64]{0:T(512)(128)(4,1)S(1)} %compare_and_fusion), kind=kLoop, calls=%fused_computation.14 | loop fusion | flops 4718592 | bytes 18874432 | tf_op jit(solution)/shard_map/jit(_where)/select_n | solution.py:102
  147.3 0.0 all-to-all-done
  147.3 10.5 %all-to-all-start.2 = ((bf16[64,2,64,576]{3,2,1,0:T(8,128)(2,1)}), bf16[64,2,64,576]{3,2,1,0:T(8,128)(2,1)}, u32[]{:S(2)}, u32[]{:S(2)}) async-start(bf16[64,2,64,576]{3,2,1,0:T(8,128)(2,1)} %broadcast_select_fusion), calls=%async_computation.2 | async-start | bytes 20971520 | tf_op jit(solution)/shard_map/all_to_all | solution.py:103
  157.8 1.5 copy.27
  159.3 229.2 %all-to-all-done.2 = bf16[64,2,64,576]{3,2,1,0:T(8,128)(2,1)} async-done(((bf16[64,2,64,576]{3,2,1,0:T(8,128)(2,1)}), bf16[64,2,64,576]{3,2,1,0:T(8,128)(2,1)}, u32[]{:S(2)}, u32[]{:S(2)}) %all-to-all-start.2) | async-done | bytes 9437216 | tf_op jit(solution)/shard_map/all_to_all | solution.py:103
  388.5 5.9 %all-to-all-start.3 = ((bf16[2,64,16,512]{3,2,0,1:T(8,128)(2,1)}), bf16[2,64,16,512]{3,2,0,1:T(8,128)(2,1)S(1)}, u32[]{:S(2)}, u32[]{:S(2)}) async-start(bf16[2,64,16,512]{3,2,0,1:T(8,128)(2,1)} %copy.27), calls=%async_computation.3 | async-start | bytes 4194304 | tf_op jit(solution)/shard_map/all_to_all | solution.py:111
  394.4 0.1 add.66
  394.5 0.1 add.67
  394.6 0.1 add.69
  394.7 0.6 dynamic-slice.2
  395.4 0.4 fusion.60
  395.8 0.2 fusion.34
  396.0 0.7 add_compare_fusion
  396.6 0.1 reduce_max.40
  396.7 5.8 %reduce_sum.67 = bf16[2,64,576]{2,1,0:T(8,128)(2,1)S(1)} reduce(bf16[64,2,64,576]{3,2,1,0:T(8,128)(2,1)} %all-to-all-done.2, bf16[]{:T(256)} %constant.15.clone.1), dimensions={0}, to_apply=%region_5.6 | reduce | flops 4644864 | bytes 9584642 | tf_op jit(solution)/shard_map/reduce_sum | solution.py:104
  402.6 0.2 fusion.61
  402.8 0.2 fusion.44
  403.0 0.1 fusion.58
  403.1 42.5 %all-to-all-done.3 = bf16[2,64,16,512]{3,2,0,1:T(8,128)(2,1)S(1)} async-done(((bf16[2,64,16,512]{3,2,0,1:T(8,128)(2,1)}), bf16[2,64,16,512]{3,2,0,1:T(8,128)(2,1)S(1)}, u32[]{:S(2)}, u32[]{:S(2)}) %all-to-all-start.3) | async-done | bytes 2097184 | tf_op jit(solution)/shard_map/all_to_all | solution.py:111
  445.6 0.5 multiply_reduce_fusion
  446.1 0.2 fusion.24
  446.3 0.9 fusion.18
  (30 shorter events, 0.1 us)
Async XLA Ops:
  6.5 93.0 %all-gather.3.cloned.1.call-start = ((), (), s32[]{:S(2)}) async-start(), calls=%async_computation.4 | async-start | bytes 2662400 | tf_op jit(solution)/shard_map/all_gather | solution.py:66
  99.5 18.8 %copy-start = (bf16[1,8,64,576]{3,2,1,0:T(8,128)(2,1)S(1)}, bf16[1,8,64,576]{3,2,1,0:T(8,128)(2,1)}, u32[]{:S(2)}) copy-start(bf16[1,8,64,576]{3,2,1,0:T(8,128)(2,1)} %param.11) | copy-start | bytes 1769476
  99.5 2.2 copy-start.1
  102.3 2.2 copy-start.1
  105.2 2.2 copy-start.1
  108.0 2.2 copy-start.1
  111.5 16.4 %all-to-all-start.1 = ((f32[2,64,16]{2,0,1:T(2,128)}), f32[2,64,16]{2,0,1:T(2,128)S(1)}, u32[]{:S(2)}, u32[]{:S(2)}) async-start(f32[2,64,16]{2,0,1:T(2,128)} %copy.23), calls=%async_computation.1 | async-start | bytes 131072 | tf_op jit(solution)/shard_map/all_to_all | solution.py:114
  127.9 19.4 %all-to-all-start = ((f32[2,64,16]{2,0,1:T(2,128)}), f32[2,64,16]{2,0,1:T(2,128)S(1)}, u32[]{:S(2)}, u32[]{:S(2)}) async-start(f32[2,64,16]{2,0,1:T(2,128)} %copy.22), calls=%async_computation | async-start | bytes 131072 | tf_op jit(solution)/shard_map/all_to_all | solution.py:115
  147.3 241.2 %all-to-all-start.2 = ((bf16[64,2,64,576]{3,2,1,0:T(8,128)(2,1)}), bf16[64,2,64,576]{3,2,1,0:T(8,128)(2,1)}, u32[]{:S(2)}, u32[]{:S(2)}) async-start(bf16[64,2,64,576]{3,2,1,0:T(8,128)(2,1)} %broadcast_select_fusion), calls=%async_computation.2 | async-start | bytes 20971520 | tf_op jit(solution)/shard_map/all_to_all | solution.py:103
  159.3 235.1 %copy-start.3 = (s32[1,2]{1,0:T(1,128)S(1)}, s32[1,2]{1,0:T(1,128)}, u32[]{:S(2)}) copy-start(s32[1,2]{1,0:T(1,128)} %param.15) | copy-start | bytes 28
  159.3 236.0 %copy-start.2 = (bf16[2,1,16,576]{3,2,1,0:T(8,128)(2,1)S(1)}, bf16[2,1,16,576]{3,2,1,0:T(8,128)(2,1)}, u32[]{:S(2)}) copy-start(bf16[2,1,16,576]{3,2,1,0:T(8,128)(2,1)} %param.9) | copy-start | bytes 110596
  159.3 236.0 %copy-start.4 = (bf16[2,1,576]{2,0,1:T(2,128)(2,1)S(1)}, bf16[2,1,576]{2,0,1:T(2,128)(2,1)}, u32[]{:S(2)}) copy-start(bf16[2,1,576]{2,0,1:T(2,128)(2,1)} %param.12) | copy-start | bytes 6916
  388.5 57.1 %all-to-all-start.3 = ((bf16[2,64,16,512]{3,2,0,1:T(8,128)(2,1)}), bf16[2,64,16,512]{3,2,0,1:T(8,128)(2,1)S(1)}, u32[]{:S(2)}, u32[]{:S(2)}) async-start(bf16[2,64,16,512]{3,2,0,1:T(8,128)(2,1)} %copy.27), calls=%async_computation.3 | async-start | bytes 4194304 | tf_op jit(solution)/shard_map/all_to_all | solution.py:111
Sparse Core Ops, SparseCore 0:
  10.6 88.8 all-gather.2
where the time goes:
time: 455 us; the launch traced here: 454 us
  waiting for transfers between devices  308 us (68%)
  blocking collectives  53.3 us (12%)
  starting transfers between devices  32.3 us (7%)
  other arithmetic  18.3 us (4%)
  local copies, waits for them, and re-layouts  15.4 us (3%)
  between operations  14.9 us (3%)
  matrix products  11.6 us (3%)
    all_to_all x1, waiting for transfers between devices, on_device(): lax.all_to_all(outgoing, 'req', split_axis=0, concat_axis=0, tiled=True)  229 us
    all_to_all x1, waiting for transfers between devices, on_device(): lax.all_to_all(out_p.astype(jnp.float32), 'req', split_axis=1, concat_axi...  42.5 us
    all_gather x1, blocking collectives, on_device(): lax.all_gather(fork_pages, 'req', axis=0, tiled=True)  39.9 us
    all_gather x1, waiting for transfers between devices, on_device(): every_query = lax.all_gather(queries, 'req', axis=1, tiled=True)  34.7 us
    unnamed x1, blocking collectives  13.4 us
    all_to_all x1, starting transfers between devices, on_device(): lax.all_to_all(outgoing, 'req', split_axis=0, concat_axis=0, tiled=True)  10.5 us
    select_n x1, other arithmetic, on_device(): jnp.where(owned[:, None, None, None], picked, jnp.zeros_like(picked))  9.98 us
    all_to_all x1, starting transfers between devices, on_device(): lax.all_to_all(total_p, 'req', split_axis=1, concat_axis=1, tiled=True)  9.44 us
  transfers between devices with their start and end apart: 5, of which 4 were waited for; matrix products, arithmetic and copies ran while one was open for 7% of the time, Pallas kernels for 0%

commit v1 on v0

--- a/solution.py
+++ b/solution.py
@@ -63,7 +63,15 @@
     forks_n = fork_pages.shape[1]
     req_n = lax.axis_size("req")
     first_beam = lax.axis_index("req") * beam_dev
-    every_query = lax.all_gather(queries, "req", axis=1, tiled=True)
+    every_query = jnp.concatenate(
+        lax.all_to_all(
+            jnp.stack([queries for _ in range(lax.axis_size("req"))], 0),
+            axis_name="req",
+            concat_axis=0,
+            split_axis=0,
+        ),
+        1,
+    )
     all_parent, all_pages, all_len = (
         lax.all_gather(parent, "req", axis=0, tiled=True),
         lax.all_gather(fork_pages, "req", axis=0, tiled=True),

time: 455 us -> 476 us (1.046)
  blocking collectives: 53.3 us -> 102 us
  waiting for transfers between devices: 308 us -> 273 us
  starting transfers between devices: 32.3 us -> 47.4 us
  between operations: 14.9 us -> 1.56 us
  local copies, waits for them, and re-layouts: 15.4 us -> 23 us
    all_gather x1, blocking collectives: 39.9 us -> 87.6 us  [on_device(): lax.all_gather(fork_pages, 'req', axis=0, tiled=True)]
    all_gather x1 -> x0, waiting for transfers between devices: 34.7 us -> none  [on_device(): every_query = lax.all_gather(queries, 'req', axis=1, tiled=True)]
    all_to_all x0 -> x1, starting transfers between devices: none -> 11.7 us  [on_device(): lax.all_to_all(jnp.stack([queries for _ in range(lax.axis_size('req'))],...]
  transfers between devices with their start and end apart: 5 -> 5, of which waited for: 4 -> 3; matrix products, arithmetic and copies ran while one was open for 7% -> 7% of each run, Pallas kernels for 0% -> 0%
where the time goes in v1:
time: 476 us
  waiting for transfers between devices  273 us (57%)
  blocking collectives  102 us (21%)
  starting transfers between devices  47.4 us (10%)
  local copies, waits for them, and re-layouts  23 us (5%)
  other arithmetic  18.3 us (4%)
  matrix products  10.7 us (2%)
    all_to_all x1, waiting for transfers between devices, on_device(): lax.all_to_all(outgoing, 'req', split_axis=0, concat_axis=0, tiled=True)  229 us
    all_gather x1, blocking collectives, on_device(): lax.all_gather(fork_pages, 'req', axis=0, tiled=True)  87.6 us
    all_to_all x1, waiting for transfers between devices, on_device(): lax.all_to_all(out_p.astype(jnp.float32), 'req', split_axis=1, concat_axi...  42.5 us
    unnamed x1, blocking collectives  14.5 us
    all_to_all x1, starting transfers between devices, on_device(): lax.all_to_all(jnp.stack([queries for _ in range(lax.axis_size('req'))],...  11.7 us
    all_to_all x1, starting transfers between devices, on_device(): lax.all_to_all(outgoing, 'req', split_axis=0, concat_axis=0, tiled=True)  10.5 us
    select_n x1, other arithmetic, on_device(): jnp.where(owned[:, None, None, None], picked, jnp.zeros_like(picked))  9.98 us
    all_to_all x1, starting transfers between devices, on_device(): lax.all_to_all(top_p, 'req', split_axis=1, concat_axis=1, tiled=True)  9.84 us
  transfers between devices with their start and end apart: 5, of which 3 were waited for; matrix products, arithmetic and copies ran while one was open for 7% of the time, Pallas kernels for 0%

profile of v1, /device:TPU:1, one launch (start us, length us, event | category | flops | bytes accessed | tf_op | source)
XLA Modules:
  0.0 475.6 jit_solution(11226184820793423930)
XLA Ops:
  0.0 2.5 stack.2
  2.5 11.7 %all-to-all-start = ((bf16[64,2,1,16,576]{4,3,1,2,0:T(8,128)(2,1)}), bf16[64,2,1,16,576]{4,3,1,2,0:T(8,128)(2,1)S(1)}, u32[]{:S(2)}, u32[]{:S(2)}) async-start(bf16[64,2,1,16,576]{4,3,1,2,0:T(8,128)(2,1)} %stack.2), calls=%async_computation | async-start | bytes 5242880 | tf_op jit(solution)/shard_map/all_to_all | solution.py:67
  15.6 87.6 %all-gather = s32[64,1,2]{2,1,0:T(1,128)S(1)} all-gather(s32[1,1,2]{2,1,0:T(1,128)S(1)} %bitcast.154), channel_id=1, replica_groups=mesh['req'=64,'head'=8] {'req'}, dimensions={0}, use_global_device_ids=true | all-gather | bytes 520 | tf_op jit(solution)/shard_map/all_gather | solution.py:77
  103.2 0.1 copy.25
  103.3 1.3 dynamic-slice.3
  104.5 0.7 dynamic-update-slice.2
  105.3 0.7 dynamic-update-slice.1
  106.0 14.5 %all-reduce.2 = (s32[64]{0:T(128)S(1)}, s32[64]{0:T(128)S(1)}) all-reduce(s32[64]{0:T(128)S(1)} %dynamic-update-slice.2, s32[64]{0:T(128)S(1)} %dynamic-update-slice.1), channel_id=1, replica_groups=mesh['req'=64,'head'=8] {'req'}, use_global_device_ids=true, to_apply=%add.1 | all-reduce | flops 128 | bytes 1024
  120.5 0.0 all-to-all-done
  120.5 1.5 copy-done.2
  122.0 3.6 copy.22
  125.7 10.3 %while.15 = (s32[]{:T(128)}, f32[4,512]{1,0:T(4,128)S(1)}, f32[4,512]{1,0:T(4,128)S(1)}, bf16[4,512,512]{2,1,0:T(8,128)(2,1)S(1)}, bf16[4,512,576]{2,1,0:T(8,128...) while((s32[]{:T(128)}, f32[4,512]{1,0:T(4,128)S(1)}, f32[4,512]{1,0:T(4,128)S(1)}, ...), condition=%wide.region_3.4_spmd, body=%wide.region_0.3_spmd.sunk | while | flops 572521472 | bytes 5458529 | solution.py:84
  125.7 1.8 fusion.73
  127.5 0.2 fusion.74
  127.7 0.5 fusion.75
  128.2 0.1 dynamic_update_slice.17
  128.2 0.1 dynamic_update_slice.16
  128.3 1.7 fusion.73
  130.0 0.2 fusion.74
  130.2 0.5 fusion.75
  130.7 0.1 dynamic_update_slice.17
  130.8 0.1 dynamic_update_slice.16
  130.8 1.7 fusion.73
  132.6 0.2 fusion.74
  132.8 0.5 fusion.75
  133.3 0.1 dynamic_update_slice.17
  133.3 0.1 dynamic_update_slice.16
  133.4 1.7 fusion.73
  135.1 0.2 fusion.74
  135.3 0.5 fusion.75
  135.8 0.1 dynamic_update_slice.17
  135.9 0.1 dynamic_update_slice.16
  135.9 0.1 reshape.290
  136.0 0.7 copy.24
  136.7 9.8 %all-to-all-start.2 = ((f32[2,64,16]{2,0,1:T(2,128)}), f32[2,64,16]{2,0,1:T(2,128)S(1)}, u32[]{:S(2)}, u32[]{:S(2)}) async-start(f32[2,64,16]{2,0,1:T(2,128)} %copy.24), calls=%async_computation.2 | async-start | bytes 131072 | tf_op jit(solution)/shard_map/all_to_all | solution.py:122
  146.6 0.1 copy.26
  146.7 0.1 reshape.321
  146.8 7.9 %gather_fusion = bf16[128,64,576]{2,1,0:T(8,128)(2,1)} fusion(bf16[1,8,64,576]{3,2,1,0:T(8,128)(2,1)S(1)} %copy-done, s32[128]{0:T(128)S(1)} %reshape.321), kind=kCustom, calls=%fused_computation | custom fusion | bytes 18875392 | tf_op jit(solution)/shard_map/gather | solution.py:91
  154.7 0.1 reshape.289
  154.8 0.7 copy.23
  155.5 0.9 all-to-all-done.2
  156.4 9.4 %all-to-all-start.1 = ((f32[2,64,16]{2,0,1:T(2,128)}), f32[2,64,16]{2,0,1:T(2,128)S(1)}, u32[]{:S(2)}, u32[]{:S(2)}) async-start(f32[2,64,16]{2,0,1:T(2,128)} %copy.23), calls=%async_computation.1 | async-start | bytes 131072 | tf_op jit(solution)/shard_map/all_to_all | solution.py:123
  165.8 10.0 %broadcast_select_fusion = bf16[64,2,64,576]{3,2,1,0:T(8,128)(2,1)} fusion(bf16[64,2,64,576]{3,2,1,0:T(8,128)(2,1)} %bitcast.145, pred[64]{0:T(512)(128)(4,1)S(1)} %compare_and_fusion), kind=kLoop, calls=%fused_computation.14 | loop fusion | flops 4718592 | bytes 18874432 | tf_op jit(solution)/shard_map/jit(_where)/select_n | solution.py:110
  175.8 0.0 all-to-all-done.1
  175.8 10.5 %all-to-all-start.3 = ((bf16[64,2,64,576]{3,2,1,0:T(8,128)(2,1)}), bf16[64,2,64,576]{3,2,1,0:T(8,128)(2,1)}, u32[]{:S(2)}, u32[]{:S(2)}) async-start(bf16[64,2,64,576]{3,2,1,0:T(8,128)(2,1)} %broadcast_select_fusion), calls=%async_computation.3 | async-start | bytes 20971520 | tf_op jit(solution)/shard_map/all_to_all | solution.py:111
  186.3 1.6 copy.28
  187.9 229.1 %all-to-all-done.3 = bf16[64,2,64,576]{3,2,1,0:T(8,128)(2,1)} async-done(((bf16[64,2,64,576]{3,2,1,0:T(8,128)(2,1)}), bf16[64,2,64,576]{3,2,1,0:T(8,128)(2,1)}, u32[]{:S(2)}, u32[]{:S(2)}) %all-to-all-start.3) | async-done | bytes 9437216 | tf_op jit(solution)/shard_map/all_to_all | solution.py:111
  417.0 5.9 %all-to-all-start.4 = ((bf16[2,64,16,512]{3,2,0,1:T(8,128)(2,1)}), bf16[2,64,16,512]{3,2,0,1:T(8,128)(2,1)S(1)}, u32[]{:S(2)}, u32[]{:S(2)}) async-start(bf16[2,64,16,512]{3,2,0,1:T(8,128)(2,1)} %copy.28), calls=%async_computation.4 | async-start | bytes 4194304 | tf_op jit(solution)/shard_map/all_to_all | solution.py:119
  422.9 0.1 add.66
  422.9 0.1 add.67
  423.0 0.1 add.69
  423.1 0.6 dynamic-slice.2
  423.8 0.4 fusion.60
  424.2 0.2 fusion.34
  424.4 0.7 add_compare_fusion
  425.1 0.1 reduce_max.40
  425.2 5.8 %reduce_sum.67 = bf16[2,64,576]{2,1,0:T(8,128)(2,1)S(1)} reduce(bf16[64,2,64,576]{3,2,1,0:T(8,128)(2,1)} %all-to-all-done.3, bf16[]{:T(256)} %constant.15.clone.1), dimensions={0}, to_apply=%region_5.6 | reduce | flops 4644864 | bytes 9584642 | tf_op jit(solution)/shard_map/reduce_sum | solution.py:112
  431.0 0.2 fusion.61
  431.3 0.2 fusion.42
  431.5 0.1 fusion.58
  431.6 42.5 %all-to-all-done.4 = bf16[2,64,16,512]{3,2,0,1:T(8,128)(2,1)S(1)} async-done(((bf16[2,64,16,512]{3,2,0,1:T(8,128)(2,1)}), bf16[2,64,16,512]{3,2,0,1:T(8,128)(2,1)S(1)}, u32[]{:S(2)}, u32[]{:S(2)}) %all-to-all-start.4) | async-done | bytes 2097184 | tf_op jit(solution)/shard_map/all_to_all | solution.py:119
  474.1 0.5 multiply_reduce_fusion
  474.5 0.2 fusion.24
  474.7 0.9 fusion.18
  (29 shorter events, 0.1 us)
Async XLA Ops:
  2.5 13.1 %copy-start.5 = (s32[1,2]{1,0:T(1,128)S(1)}, s32[1,2]{1,0:T(1,128)}, u32[]{:S(2)}) copy-start(s32[1,2]{1,0:T(1,128)} %param.15) | copy-start | bytes 28
  2.5 118.0 %all-to-all-start = ((bf16[64,2,1,16,576]{4,3,1,2,0:T(8,128)(2,1)}), bf16[64,2,1,16,576]{4,3,1,2,0:T(8,128)(2,1)S(1)}, u32[]{:S(2)}, u32[]{:S(2)}) async-start(bf16[64,2,1,16,576]{4,3,1,2,0:T(8,128)(2,1)} %stack.2), calls=%async_computation | async-start | bytes 5242880 | tf_op jit(solution)/shard_map/all_to_all | solution.py:67
  120.5 1.5 copy-start.2
  122.0 3.6 copy-start.1
  122.0 3.6 copy-start.3
  125.7 21.2 %copy-start = (bf16[1,8,64,576]{3,2,1,0:T(8,128)(2,1)S(1)}, bf16[1,8,64,576]{3,2,1,0:T(8,128)(2,1)}, u32[]{:S(2)}) copy-start(bf16[1,8,64,576]{3,2,1,0:T(8,128)(2,1)} %param.11) | copy-start | bytes 1769476
  136.7 19.7 %all-to-all-start.2 = ((f32[2,64,16]{2,0,1:T(2,128)}), f32[2,64,16]{2,0,1:T(2,128)S(1)}, u32[]{:S(2)}, u32[]{:S(2)}) async-start(f32[2,64,16]{2,0,1:T(2,128)} %copy.24), calls=%async_computation.2 | async-start | bytes 131072 | tf_op jit(solution)/shard_map/all_to_all | solution.py:122
  156.4 19.4 %all-to-all-start.1 = ((f32[2,64,16]{2,0,1:T(2,128)}), f32[2,64,16]{2,0,1:T(2,128)S(1)}, u32[]{:S(2)}, u32[]{:S(2)}) async-start(f32[2,64,16]{2,0,1:T(2,128)} %copy.23), calls=%async_computation.1 | async-start | bytes 131072 | tf_op jit(solution)/shard_map/all_to_all | solution.py:123
  175.8 241.2 %all-to-all-start.3 = ((bf16[64,2,64,576]{3,2,1,0:T(8,128)(2,1)}), bf16[64,2,64,576]{3,2,1,0:T(8,128)(2,1)}, u32[]{:S(2)}, u32[]{:S(2)}) async-start(bf16[64,2,64,576]{3,2,1,0:T(8,128)(2,1)} %broadcast_select_fusion), calls=%async_computation.3 | async-start | bytes 20971520 | tf_op jit(solution)/shard_map/all_to_all | solution.py:111
  187.9 235.9 %copy-start.4 = (bf16[2,1,16,576]{3,2,1,0:T(8,128)(2,1)S(1)}, bf16[2,1,16,576]{3,2,1,0:T(8,128)(2,1)}, u32[]{:S(2)}) copy-start(bf16[2,1,16,576]{3,2,1,0:T(8,128)(2,1)} %param.9) | copy-start | bytes 110596
  187.9 236.0 %copy-start.6 = (bf16[2,1,576]{2,0,1:T(2,128)(2,1)S(1)}, bf16[2,1,576]{2,0,1:T(2,128)(2,1)}, u32[]{:S(2)}) copy-start(bf16[2,1,576]{2,0,1:T(2,128)(2,1)} %param.12) | copy-start | bytes 6916
  417.0 57.1 %all-to-all-start.4 = ((bf16[2,64,16,512]{3,2,0,1:T(8,128)(2,1)}), bf16[2,64,16,512]{3,2,0,1:T(8,128)(2,1)S(1)}, u32[]{:S(2)}, u32[]{:S(2)}) async-start(bf16[2,64,16,512]{3,2,0,1:T(8,128)(2,1)} %copy.28), calls=%async_computation.4 | async-start | bytes 4194304 | tf_op jit(solution)/shard_map/all_to_all | solution.py:119
